TPU v7x, 512 devices: a whole 4x8x8 slice. The times are simulated.
512 devices in a mesh: ulysses: 8 (over z_hi, x), context: 64 (over y, z_lo, core).
Axes of the slice: x: 4, y: 8, z: 8 (z_hi: 2, z_lo: 4; z = z_hi * 4 + z_lo), core: 2. Of those that a mesh axis runs over, the one named last changes fastest.
Arguments:
- queries: bfloat16 [49152, 5120], P(('context', 'ulysses')), may hold values from -7 to 7
- key_vectors: bfloat16 [49152, 5120], P(('context', 'ulysses')), may hold values from -7 to 7
- value_vectors: bfloat16 [49152, 5120], P(('context', 'ulysses')), may hold values from -6 to 6
- labels: int32 [40], replicated, may hold values from 0 to 1, as said below
- block_lists: int32 [40, 768, 5], replicated, may hold values from 0 to 767, as said below
- counts: int32 [40, 768], replicated, may hold values from 1 to 5, as said below
- query_scale: float32 [40], replicated, may hold values from 1.5 to 3
- key_scale: float32 [40], replicated, may hold values from 1.5 to 3
- value_scale: float32 [40], replicated, may hold values from 0.5 to 2
Outputs:
- attended: bfloat16 [49152, 5120], P(('context', 'ulysses'))
Inputs may be any that keep to these rules, and one draw needn't show every extreme that they name: `labels`: exactly 16 entries are 1, the others 0; every aligned run of 5 heads holds at least one 0. Every entry of block_lists[h, b] lies within 2 blocks of b; the first entry is b itself and the first counts[h, b] entries are distinct. counts[h, b] is at least one less than and at most the number of blocks of the clip within 2 blocks of b; every head has a query block that uses all 5 entries.
All inputs are finite; a program needn't handle non-finite values.
Results may differ from a plain program's by a relative error of at most 0.0024.
Values may be sent and summed in bfloat16 or wider, within the bound.
No kernel may reach another device: no remote copies, remote signals or barrier semaphores. Data moves between devices by JAX's collectives and lax.ppermute only.
A program may use at most 128 MiB of HBM per device.

v0:
```python
import math
import jax
import jax.numpy as jnp
from jax import lax
from jax.sharding import Mesh, PartitionSpec as P

FRAMES = 16
MARGIN = 2
BLOCK = 64


def with_halo(cells, axes, order):
    width = MARGIN * BLOCK
    pairs = list(zip(order[:-1], order[1:]))
    lower = lax.ppermute(cells[-width:], axes, pairs)
    upper = lax.ppermute(cells[:width], axes, [(b, a) for a, b in pairs])
    return jnp.concatenate([lower, cells, upper], axis=0)


def window_mask(block_lists, counts, head_ids, base, blocks):
    span = 2 * MARGIN + 1
    list_length = block_lists.shape[2]
    head_lists = jnp.take(block_lists, head_ids, axis=0)
    head_counts = jnp.take(counts, head_ids, axis=0)
    global_ids = base[:, None] + jnp.arange(blocks, dtype=jnp.int32)[None, :]
    lists = jnp.take_along_axis(head_lists, global_ids[:, :, None], axis=1)
    used = jnp.take_along_axis(head_counts, global_ids, axis=1)
    wanted = global_ids[:, :, None] + jnp.arange(span, dtype=jnp.int32)[None, None, :] - MARGIN
    live = jnp.arange(list_length, dtype=jnp.int32)[None, None, :] < used[:, :, None]
    hit = (lists[:, :, None, :] == wanted[:, :, :, None]) & live[:, :, None, :]
    return jnp.any(hit, axis=-1)


def attend(query_rows, key_ext, value_ext, allowed, logit_scale, value_factor):
    rows, heads, width = query_rows.shape
    blocks = rows // BLOCK
    span = 2 * MARGIN + 1
    q = query_rows.reshape(blocks, BLOCK, heads, width)
    kb = key_ext.reshape(blocks + 2 * MARGIN, BLOCK, heads, width)
    vb = value_ext.reshape(blocks + 2 * MARGIN, BLOCK, heads, width)
    kw = jnp.stack([kb[o : o + blocks] for o in range(span)], axis=1)
    vw = jnp.stack([vb[o : o + blocks] for o in range(span)], axis=1)
    logits = jnp.einsum("bqhd,bokhd->hbqok", q, kw, preferred_element_type=jnp.float32)
    logits = logits * logit_scale[:, None, None, None, None]
    logits = jnp.where(allowed[:, :, None, :, None], logits, -jnp.inf)
    peak = jnp.max(logits, axis=(3, 4), keepdims=True)
    weight = jnp.exp(logits - peak)
    total = jnp.sum(weight, axis=(3, 4))
    mixed = jnp.einsum(
        "hbqok,bokhd->bqhd", weight.astype(jnp.bfloat16), vw, preferred_element_type=jnp.float32
    )
    factor = value_factor[:, None, None] / total
    out = mixed * jnp.transpose(factor, (1, 2, 0))[:, :, :, None]
    return out.astype(jnp.bfloat16).reshape(rows, heads, width)


def shards(
    queries,
    key_vectors,
    value_vectors,
    labels,
    block_lists,
    counts,
    query_scale,
    key_scale,
    value_scale,
):
    groups = lax.axis_size("ulysses")
    frames = lax.axis_size("frame")
    quarters = lax.axis_size("quarter")
    devices_along = frames * quarters
    tokens_here = queries.shape[0]
    head_count = labels.shape[0]
    width = queries.shape[1] // head_count
    per_group = head_count // groups
    rows = tokens_here * groups
    blocks = rows // BLOCK
    piece = rows // frames
    group_index = lax.axis_index("ulysses")
    frame_index = lax.axis_index("frame")
    quarter_index = lax.axis_index("quarter")
    spatial_slot = frame_index * quarters + quarter_index
    temporal_slot = quarter_index * frames + frame_index
    stacked = jnp.concatenate(
        [
            queries.reshape(tokens_here, groups, per_group, width),
            key_vectors.reshape(tokens_here, groups, per_group, width),
            value_vectors.reshape(tokens_here, groups, per_group, width),
        ],
        axis=2,
    )
    frame_rows = lax.all_to_all(stacked, "ulysses", split_axis=1, concat_axis=0, tiled=True)
    frame_rows = frame_rows.reshape(rows, 3 * per_group, width)
    moved = lax.all_to_all(
        frame_rows.reshape(frames, piece, 3 * per_group, width),
        "frame",
        split_axis=0,
        concat_axis=0,
        tiled=True,
    )
    line_rows = jnp.transpose(moved, (1, 0, 2, 3)).reshape(rows, 3 * per_group, width)
    spatial_order = list(range(devices_along))
    temporal_order = [k % frames * quarters + k // frames for k in range(devices_along)]
    frame_ext = with_halo(frame_rows[:, per_group:], ("frame", "quarter"), spatial_order)
    line_ext = with_halo(line_rows[:, per_group:], ("frame", "quarter"), temporal_order)
    head_ids = group_index * per_group + jnp.arange(per_group, dtype=jnp.int32)
    temporal = jnp.take(labels, head_ids) == 1
    doubled = jnp.concatenate([temporal, temporal])
    query_rows = jnp.where(
        temporal[None, :, None], line_rows[:, :per_group], frame_rows[:, :per_group]
    )
    extended = jnp.where(doubled[None, :, None], line_ext, frame_ext)
    base = jnp.where(temporal, temporal_slot * blocks, spatial_slot * blocks).astype(jnp.int32)
    allowed = window_mask(block_lists, counts, head_ids, base, blocks)
    logit_scale = jnp.take(query_scale, head_ids) * jnp.take(key_scale, head_ids) / math.sqrt(width)
    value_factor = jnp.take(value_scale, head_ids)
    outputs = attend(
        query_rows,
        extended[:, :per_group],
        extended[:, per_group:],
        allowed,
        logit_scale,
        value_factor,
    )
    back = jnp.transpose(outputs.reshape(piece, frames, per_group, width), (1, 0, 2, 3))
    returned = lax.all_to_all(back, "frame", split_axis=0, concat_axis=0, tiled=True)
    returned = returned.reshape(rows, per_group, width)
    frame_outputs = jnp.where(temporal[None, :, None], returned, outputs)
    merged = lax.all_to_all(
        frame_outputs.reshape(rows, 1, per_group, width),
        "ulysses",
        split_axis=0,
        concat_axis=1,
        tiled=True,
    )
    return merged.reshape(tokens_here, head_count * width)


def solution(mesh):
    ulysses, context = mesh.devices.shape
    fine = Mesh(
        mesh.devices.reshape(ulysses, FRAMES, context // FRAMES), ("ulysses", "frame", "quarter")
    )
    rows = P(("frame", "quarter", "ulysses"), None)
    placed = (rows, rows, rows, P(), P(), P(), P(), P(), P())
    return jax.shard_map(shards, mesh=fine, in_specs=placed, out_specs=rows, check_vma=False)
```

profile of v0, /device:TPU:48, one launch (start us, length us, event | category | flops | bytes accessed | tf_op | source)
XLA Modules:
  0.0 332.7 jit_solution(10874801442408721896)
XLA Ops:
  0.0 1.8 copy.74
  1.8 1.7 copy.75
  3.5 2.4 copy.76
  5.9 3.4 %pad_maximum_fusion = bf16[96,8,15,128]{0,3,2,1:T(8,128)(2,1)} fusion(bf16[96,8,5,128]{0,3,2,1:T(8,128)(2,1)} %bitcast.67, bf16[96,8,5,128]{0,3,2,1:T(8,128)(2,1)S(1)} %bitcast.66, bf16[96,8,5,128]{0,3,2,1:T(8,128)(2,1)S(1)} %bitcast.65), kind=kLoop, calls=%fused_computation.16 | loop fusion | flops 2949120 | bytes 5898240 | tf_op jit(solution)/shard_map/concatenate | solution.py:84
  9.3 5.8 %copy.77 = bf16[96,8,15,128]{3,0,2,1:T(8,128)(2,1)} copy(bf16[96,8,15,128]{0,3,2,1:T(8,128)(2,1)} %pad_maximum_fusion) | data formatting | bytes 5898240 | tf_op jit(solution)/shard_map/concatenate | solution.py:84
  15.0 82.2 %all_to_all.40 = bf16[96,8,15,128]{3,0,2,1:T(8,128)(2,1)S(1)} all-to-all(bf16[96,8,15,128]{3,0,2,1:T(8,128)(2,1)} %copy.77), channel_id=1, replica_groups=mesh['ulysses'=8,'frame'=16,'quarter'=4] {'ulysses'}, dimensions={1} | all-to-all | bytes 5898240 | tf_op jit(solution)/shard_map/all_to_all | solution.py:92
  97.2 0.3 copy.78
  97.5 1.6 copy-done.6
  99.1 2.2 copy.79
  101.3 11.1 %all-to-all-start.1 = ((bf16[16,48,15,128]{3,1,2,0:T(8,128)(2,1)}), bf16[16,48,15,128]{3,1,2,0:T(8,128)(2,1)}, u32[]{:S(2)}, u32[]{:S(2)}) async-start(bf16[16,48,15,128]{3,1,2,0:T(8,128)(2,1)} %copy.79), calls=%async_computation.1 | async-start | bytes 5898240 | tf_op jit(solution)/shard_map/all_to_all | solution.py:94
  112.4 0.6 gather_fusion.7
  113.0 0.6 gather_fusion.6
  113.7 0.6 gather_fusion.5
  114.4 0.6 gather_fusion
  115.2 0.6 gather_fusion.2
  115.8 1.0 gather_fusion.4
  116.9 0.7 gather_fusion.1
  117.7 0.6 copy.86
  118.3 1.1 gather_fusion.3
  119.8 1.1 fusion.16
  121.0 1.9 collective-permute-start.2
  122.9 6.3 %collective-permute-start.3 = (bf16[128,10,128]{2,0,1:T(8,128)(2,1)S(1)}, bf16[128,10,128]{2,0,1:T(8,128)(2,1)S(1)}, u32[]{:S(2)}, u32[]{:S(2)}) collective-permute-start(bf16[128,10,128]{2,0,1:T(8,128)(2,1)S(1)} %get-tuple-element.11), channel_id=1, source_target_pairs={{1,0},{2,1},{3,2},{4,3},{5,4},{6,5},{7,6},{8,7},{9,8},{10,9},{11,1... | collective-permute-start | bytes 983048 | tf_op jit(solution)/shard_map/ppermute | solution.py:16
  129.2 82.6 %all-to-all-done.1 = bf16[16,48,15,128]{3,1,2,0:T(8,128)(2,1)} async-done(((bf16[16,48,15,128]{3,1,2,0:T(8,128)(2,1)}), bf16[16,48,15,128]{3,1,2,0:T(8,128)(2,1)}, u32[]{:S(2)}, u32[]{:S(2)}) %all-to-all-start.1) | async-done | bytes 2949152 | tf_op jit(solution)/shard_map/all_to_all | solution.py:94
  211.8 2.6 copy.80
  214.4 1.6 copy-done.7
  216.1 1.9 collective-permute-start
  218.0 5.9 %collective-permute-start.1 = (bf16[128,10,128]{2,0,1:T(8,128)(2,1)S(1)}, bf16[128,10,128]{2,0,1:T(8,128)(2,1)S(1)}, u32[]{:S(2)}, u32[]{:S(2)}) collective-permute-start(bf16[128,10,128]{2,0,1:T(8,128)(2,1)S(1)} %get-tuple-element.13), channel_id=1, source_target_pairs={{4,0},{8,4},{12,8},{16,12},{20,16},{24,20},{28,24},{32,28},{36,32}... | collective-permute-start | bytes 983048 | tf_op jit(solution)/shard_map/ppermute | solution.py:16
  224.0 0.1 copy.89
  224.1 1.9 slice.118
  226.0 0.6 copy-done.8
  226.6 0.1 slice.115
  226.7 1.4 slice_select_fusion
  228.1 6.4 %collective-permute-done = bf16[128,10,128]{2,0,1:T(8,128)(2,1)S(1)} collective-permute-done((bf16[128,10,128]{2,0,1:T(8,128)(2,1)S(1)}, bf16[128,10,128]{2,0,1:T(8,128)(2,1)S(1)}, u32[]{:S(2)}, u32[]{:S(2)}) %collective-permute-start) | collective-permute-done | bytes 327712 | tf_op jit(solution)/shard_map/ppermute | solution.py:15
  234.5 11.7 %collective-permute-done.1 = bf16[128,10,128]{2,0,1:T(8,128)(2,1)S(1)} collective-permute-done((bf16[128,10,128]{2,0,1:T(8,128)(2,1)S(1)}, bf16[128,10,128]{2,0,1:T(8,128)(2,1)S(1)}, u32[]{:S(2)}, u32[]{:S(2)}) %collective-permute-start.1) | collective-permute-done | bytes 327712 | tf_op jit(solution)/shard_map/ppermute | solution.py:16
  246.2 0.8 maximum_select_fusion
  247.1 0.8 fusion.18
  248.3 0.1 constant_dynamic-update-slice_fusion.6
  248.5 1.5 fusion
  250.1 3.0 fusion.1
  253.8 2.1 fusion.6
  255.9 0.3 copy.93
  256.2 31.2 %all_to_all.41 = bf16[16,48,5,128]{3,1,2,0:T(8,128)(2,1)S(1)} all-to-all(bf16[16,48,5,128]{3,1,2,0:T(8,128)(2,1)S(1)} %copy.93), channel_id=1, replica_groups=mesh['ulysses'=8,'frame'=16,'quarter'=4] {'frame'}, dimensions={0} | all-to-all | bytes 1966080 | tf_op jit(solution)/shard_map/all_to_all | solution.py:126
  287.5 0.2 bitcast_select_fusion
  287.7 0.7 copy.96
  288.5 42.0 %all_to_all.42 = bf16[768,1,5,128]{3,2,1,0:T(8,128)(2,1)S(1)} all-to-all(bf16[768,1,5,128]{3,2,1,0:T(8,128)(2,1)S(1)} %copy.96), channel_id=1, replica_groups=mesh['ulysses'=8,'frame'=16,'quarter'=4] {'ulysses'}, dimensions={0} | all-to-all | bytes 1966080 | tf_op jit(solution)/shard_map/all_to_all | solution.py:129
  330.5 0.1 copy.97
  330.6 0.8 copy.98
  331.4 1.4 copy.99
  (55 shorter events, 2.3 us)
Async XLA Ops:
  0.0 116.9 %copy-start = (s32[40,768,5]{1,0,2:T(8,128)S(1)}, s32[40,768,5]{1,0,2:T(8,128)}, u32[]{:S(2)}) copy-start(s32[40,768,5]{1,0,2:T(8,128)} %param.15) | copy-start | bytes 1843204
  97.5 1.6 copy-start.6
  99.1 13.3 %copy-start.2 = (f32[40]{0:T(128)S(1)}, f32[40]{0:T(128)}, u32[]{:S(2)}) copy-start(f32[40]{0:T(128)} %param.19) | copy-start | bytes 484
  99.1 13.9 %copy-start.3 = (f32[40]{0:T(128)S(1)}, f32[40]{0:T(128)}, u32[]{:S(2)}) copy-start(f32[40]{0:T(128)} %param.18) | copy-start | bytes 484
  101.3 12.4 %copy-start.4 = (f32[40]{0:T(128)S(1)}, f32[40]{0:T(128)}, u32[]{:S(2)}) copy-start(f32[40]{0:T(128)} %param.17) | copy-start | bytes 484
  101.3 13.1 %copy-start.5 = (s32[40]{0:T(128)S(1)}, s32[40]{0:T(128)}, u32[]{:S(2)}) copy-start(s32[40]{0:T(128)} %param.14) | copy-start | bytes 484
  101.3 13.9 %copy-start.9 = (s32[40,768]{1,0:T(8,128)S(1)}, s32[40,768]{1,0:T(8,128)}, u32[]{:S(2)}) copy-start(s32[40,768]{1,0:T(8,128)} %param.16) | copy-start | bytes 368644
  101.3 110.5 %all-to-all-start.1 = ((bf16[16,48,15,128]{3,1,2,0:T(8,128)(2,1)}), bf16[16,48,15,128]{3,1,2,0:T(8,128)(2,1)}, u32[]{:S(2)}, u32[]{:S(2)}) async-start(bf16[16,48,15,128]{3,1,2,0:T(8,128)(2,1)} %copy.79), calls=%async_computation.1 | async-start | bytes 5898240 | tf_op jit(solution)/shard_map/all_to_all | solution.py:94
  121.0 107.1 %collective-permute-start.2 = (bf16[128,10,128]{2,0,1:T(8,128)(2,1)S(1)}, bf16[128,10,128]{2,0,1:T(8,128)(2,1)S(1)}, u32[]{:S(2)}, u32[]{:S(2)}) collective-permute-start(bf16[128,10,128]{2,0,1:T(8,128)(2,1)S(1)} %get-tuple-element.10), channel_id=1, source_target_pairs={{0,1},{1,2},{2,3},{3,4},{4,5},{5,6},{6,7},{7,8},{8,9},{9,10},{10,1... | collective-permute-start | bytes 983048 | tf_op jit(solution)/shard_map/ppermute | solution.py:15
  122.9 105.2 %collective-permute-start.3 = (bf16[128,10,128]{2,0,1:T(8,128)(2,1)S(1)}, bf16[128,10,128]{2,0,1:T(8,128)(2,1)S(1)}, u32[]{:S(2)}, u32[]{:S(2)}) collective-permute-start(bf16[128,10,128]{2,0,1:T(8,128)(2,1)S(1)} %get-tuple-element.11), channel_id=1, source_target_pairs={{1,0},{2,1},{3,2},{4,3},{5,4},{6,5},{7,6},{8,7},{9,8},{10,9},{11,1... | collective-permute-start | bytes 983048 | tf_op jit(solution)/shard_map/ppermute | solution.py:16
  214.4 1.6 copy-start.7
  216.1 18.4 %collective-permute-start = (bf16[128,10,128]{2,0,1:T(8,128)(2,1)S(1)}, bf16[128,10,128]{2,0,1:T(8,128)(2,1)S(1)}, u32[]{:S(2)}, u32[]{:S(2)}) collective-permute-start(bf16[128,10,128]{2,0,1:T(8,128)(2,1)S(1)} %get-tuple-element.12), channel_id=1, source_target_pairs={{0,4},{4,8},{8,12},{12,16},{16,20},{20,24},{24,28},{28,32},{32,36}... | collective-permute-start | bytes 983048 | tf_op jit(solution)/shard_map/ppermute | solution.py:15
  218.0 28.2 %collective-permute-start.1 = (bf16[128,10,128]{2,0,1:T(8,128)(2,1)S(1)}, bf16[128,10,128]{2,0,1:T(8,128)(2,1)S(1)}, u32[]{:S(2)}, u32[]{:S(2)}) collective-permute-start(bf16[128,10,128]{2,0,1:T(8,128)(2,1)S(1)} %get-tuple-element.13), channel_id=1, source_target_pairs={{4,0},{8,4},{12,8},{16,12},{20,16},{24,20},{28,24},{32,28},{36,32}... | collective-permute-start | bytes 983048 | tf_op jit(solution)/shard_map/ppermute | solution.py:16
  224.1 2.4 copy-start.8
  287.7 45.0 %copy-start.1 = (s32[40,768,5]{1,0,2:T(8,128)S(1)}, s32[40,768,5]{1,0,2:T(8,128)}, u32[]{:S(2)}) copy-start(s32[40,768,5]{1,0,2:T(8,128)} %param.15) | copy-start | bytes 1843204
where the time goes:
time: 333 us
  blocking collectives  155 us (47%)
  waiting for transfers between devices  101 us (30%)
  local copies, waits for them, and re-layouts  36 us (11%)
  starting transfers between devices  27.2 us (8%)
  other arithmetic  9.46 us (3%)
  matrix products  3.6 us (1%)
    all_to_all x1, waiting for transfers between devices, shards(): lax.all_to_all(frame_rows.reshape(frames, piece, 3 * per_group, width), '...  82.6 us
    all_to_all x1, blocking collectives, shards(): lax.all_to_all(stacked, 'ulysses', split_axis=1, concat_axis=0, tiled=True)  82.2 us
    all_to_all x1, blocking collectives, shards(): lax.all_to_all(frame_outputs.reshape(rows, 1, per_group, width), 'ulysses...  42 us
    all_to_all x1, blocking collectives, shards(): lax.all_to_all(back, 'frame', split_axis=0, concat_axis=0, tiled=True)  31.2 us
    ppermute x2, starting transfers between devices, with_halo(): upper = lax.ppermute(cells[:width], axes, [(b, a) for a, b in pairs])  12.2 us
    ppermute x2, waiting for transfers between devices, with_halo(): upper = lax.ppermute(cells[:width], axes, [(b, a) for a, b in pairs])  11.7 us
    all_to_all x1, starting transfers between devices, shards(): lax.all_to_all(frame_rows.reshape(frames, piece, 3 * per_group, width), '...  11.1 us
    unnamed x31, local copies, waits for them, and re-layouts  10.6 us
  transfers between devices with their start and end apart: 5, of which 3 were waited for; matrix products, arithmetic and copies ran while one was open for 4% of the time, Pallas kernels for 0%

commit v1 on v0

--- a/solution.py
+++ b/solution.py
@@ -126,13 +126,10 @@
     returned = lax.all_to_all(back, "frame", split_axis=0, concat_axis=0, tiled=True)
     returned = returned.reshape(rows, per_group, width)
     frame_outputs = jnp.where(temporal[None, :, None], returned, outputs)
-    merged = lax.all_to_all(
-        frame_outputs.reshape(rows, 1, per_group, width),
-        "ulysses",
-        split_axis=0,
-        concat_axis=1,
-        tiled=True,
-    )
+    block = frame_outputs.reshape(rows, 1, per_group, width)
+    parts = jnp.split(block, lax.axis_size("ulysses"), axis=0)
+    got = lax.all_to_all(jnp.stack(parts), "ulysses", 0, 0)
+    merged = jnp.concatenate(got, axis=1)
     return merged.reshape(tokens_here, head_count * width)
 
 

time: 333 us -> 320 us (0.961)
  the two profiles are of different devices: /device:TPU:48 before, /device:TPU:128 now
where the time goes in v1:
time: 320 us; the launch traced here: 319 us
  blocking collectives  154 us (48%)
  waiting for transfers between devices  94.2 us (29%)
  local copies, waits for them, and re-layouts  35.3 us (11%)
  starting transfers between devices  22.1 us (7%)
  other arithmetic  9.46 us (3%)
  matrix products  3.6 us (1%)
    all_to_all x1, blocking collectives, shards(): lax.all_to_all(stacked, 'ulysses', split_axis=1, concat_axis=0, tiled=True)  82.5 us
    all_to_all x1, waiting for transfers between devices, shards(): lax.all_to_all(frame_rows.reshape(frames, piece, 3 * per_group, width), '...  76.7 us
    all_to_all x1, blocking collectives, shards(): lax.all_to_all(back, 'frame', split_axis=0, concat_axis=0, tiled=True)  41.4 us
    all_to_all x1, blocking collectives, shards(): got = lax.all_to_all(jnp.stack(parts), 'ulysses', 0, 0)  30.3 us
    unnamed x38, local copies, waits for them, and re-layouts  10.7 us
    ppermute x2, waiting for transfers between devices, with_halo(): lower = lax.ppermute(cells[-width:], axes, pairs)  10.6 us
    all_to_all x1, starting transfers between devices, shards(): lax.all_to_all(frame_rows.reshape(frames, piece, 3 * per_group, width), '...  9.61 us
    ppermute x2, starting transfers between devices, with_halo(): upper = lax.ppermute(cells[:width], axes, [(b, a) for a, b in pairs])  8.66 us
  transfers between devices with their start and end apart: 5, of which 3 were waited for; matrix products, arithmetic and copies ran while one was open for 5% of the time, Pallas kernels for 0%

profile of v1, /device:TPU:128, one launch (start us, length us, event | category | flops | bytes accessed | tf_op | source)
XLA Modules:
  0.0 319.3 jit_solution(8594840234909292795)
XLA Ops:
  0.0 1.8 copy.74
  1.8 1.7 copy.75
  3.5 2.4 copy.76
  5.9 3.4 %pad_maximum_fusion = bf16[96,8,15,128]{0,3,2,1:T(8,128)(2,1)} fusion(bf16[96,8,5,128]{0,3,2,1:T(8,128)(2,1)} %bitcast.97, bf16[96,8,5,128]{0,3,2,1:T(8,128)(2,1)S(1)} %bitcast.96, bf16[96,8,5,128]{0,3,2,1:T(8,128)(2,1)S(1)} %bitcast.95), kind=kLoop, calls=%fused_computation.16 | loop fusion | flops 2949120 | bytes 5898240 | tf_op jit(solution)/shard_map/concatenate | solution.py:84
  9.3 5.8 %copy.77 = bf16[96,8,15,128]{3,0,2,1:T(8,128)(2,1)} copy(bf16[96,8,15,128]{0,3,2,1:T(8,128)(2,1)} %pad_maximum_fusion) | data formatting | bytes 5898240 | tf_op jit(solution)/shard_map/concatenate | solution.py:84
  15.0 82.5 %all_to_all.30 = bf16[96,8,15,128]{3,0,2,1:T(8,128)(2,1)S(1)} all-to-all(bf16[96,8,15,128]{3,0,2,1:T(8,128)(2,1)} %copy.77), channel_id=1, replica_groups=mesh['ulysses'=8,'frame'=16,'quarter'=4] {'ulysses'}, dimensions={1} | all-to-all | bytes 5898240 | tf_op jit(solution)/shard_map/all_to_all | solution.py:92
  97.5 0.3 copy.78
  97.8 1.6 copy-done.6
  99.4 2.2 copy.79
  101.6 9.6 %all-to-all-start.1 = ((bf16[16,48,15,128]{3,1,2,0:T(8,128)(2,1)}), bf16[16,48,15,128]{3,1,2,0:T(8,128)(2,1)}, u32[]{:S(2)}, u32[]{:S(2)}) async-start(bf16[16,48,15,128]{3,1,2,0:T(8,128)(2,1)} %copy.79), calls=%async_computation.1 | async-start | bytes 5898240 | tf_op jit(solution)/shard_map/all_to_all | solution.py:94
  111.2 0.6 gather_fusion.7
  111.9 0.6 gather_fusion.6
  112.5 0.6 gather_fusion.5
  113.2 0.6 gather_fusion
  114.0 0.6 gather_fusion.2
  114.7 1.0 gather_fusion.4
  115.7 0.7 gather_fusion.1
  116.5 0.6 copy.86
  117.2 1.1 gather_fusion.3
  118.7 1.1 fusion.24
  119.8 1.9 collective-permute-start.2
  121.7 3.6 %collective-permute-start.3 = (bf16[128,10,128]{2,0,1:T(8,128)(2,1)S(1)}, bf16[128,10,128]{2,0,1:T(8,128)(2,1)S(1)}, u32[]{:S(2)}, u32[]{:S(2)}) collective-permute-start(bf16[128,10,128]{2,0,1:T(8,128)(2,1)S(1)} %get-tuple-element.11), channel_id=1, source_target_pairs={{1,0},{2,1},{3,2},{4,3},{5,4},{6,5},{7,6},{8,7},{9,8},{10,9},{11,1... | collective-permute-start | bytes 983048 | tf_op jit(solution)/shard_map/ppermute | solution.py:16
  125.4 76.7 %all-to-all-done.1 = bf16[16,48,15,128]{3,1,2,0:T(8,128)(2,1)} async-done(((bf16[16,48,15,128]{3,1,2,0:T(8,128)(2,1)}), bf16[16,48,15,128]{3,1,2,0:T(8,128)(2,1)}, u32[]{:S(2)}, u32[]{:S(2)}) %all-to-all-start.1) | async-done | bytes 2949152 | tf_op jit(solution)/shard_map/all_to_all | solution.py:94
  202.1 2.6 copy.80
  204.7 1.6 copy-done.7
  206.3 1.9 collective-permute-start
  208.2 5.0 %collective-permute-start.1 = (bf16[128,10,128]{2,0,1:T(8,128)(2,1)S(1)}, bf16[128,10,128]{2,0,1:T(8,128)(2,1)S(1)}, u32[]{:S(2)}, u32[]{:S(2)}) collective-permute-start(bf16[128,10,128]{2,0,1:T(8,128)(2,1)S(1)} %get-tuple-element.13), channel_id=1, source_target_pairs={{4,0},{8,4},{12,8},{16,12},{20,16},{24,20},{28,24},{32,28},{36,32}... | collective-permute-start | bytes 983048 | tf_op jit(solution)/shard_map/ppermute | solution.py:16
  213.3 0.1 copy.89
  213.5 1.9 slice.126
  215.3 0.6 copy-done.8
  215.9 0.1 slice.123
  216.0 1.4 slice_select_fusion
  217.4 10.6 %collective-permute-done = bf16[128,10,128]{2,0,1:T(8,128)(2,1)S(1)} collective-permute-done((bf16[128,10,128]{2,0,1:T(8,128)(2,1)S(1)}, bf16[128,10,128]{2,0,1:T(8,128)(2,1)S(1)}, u32[]{:S(2)}, u32[]{:S(2)}) %collective-permute-start) | collective-permute-done | bytes 327712 | tf_op jit(solution)/shard_map/ppermute | solution.py:15
  228.0 6.9 %collective-permute-done.1 = bf16[128,10,128]{2,0,1:T(8,128)(2,1)S(1)} collective-permute-done((bf16[128,10,128]{2,0,1:T(8,128)(2,1)S(1)}, bf16[128,10,128]{2,0,1:T(8,128)(2,1)S(1)}, u32[]{:S(2)}, u32[]{:S(2)}) %collective-permute-start.1) | collective-permute-done | bytes 327712 | tf_op jit(solution)/shard_map/ppermute | solution.py:16
  234.9 0.8 maximum_select_fusion
  235.8 0.8 fusion.26
  236.7 0.1 constant_dynamic-update-slice_fusion.8
  236.9 0.1 constant_dynamic-update-slice_fusion.7
  237.0 0.1 constant_dynamic-update-slice_fusion.6
  237.3 1.5 fusion
  238.8 3.0 fusion.1
  242.6 2.1 fusion.6
  244.7 0.3 copy.93
  245.0 41.4 %all_to_all.31 = bf16[16,48,5,128]{3,1,2,0:T(8,128)(2,1)S(1)} all-to-all(bf16[16,48,5,128]{3,1,2,0:T(8,128)(2,1)S(1)} %copy.93), channel_id=1, replica_groups=mesh['ulysses'=8,'frame'=16,'quarter'=4] {'frame'}, dimensions={0} | all-to-all | bytes 1966080 | tf_op jit(solution)/shard_map/all_to_all | solution.py:126
  286.4 0.2 bitcast_select_fusion
  286.9 30.3 %all_to_all.32 = bf16[8,96,1,5,128]{4,1,3,2,0:T(8,128)(2,1)S(1)} all-to-all(bf16[8,96,1,5,128]{4,1,3,2,0:T(8,128)(2,1)S(1)} %fusion.11), channel_id=1, replica_groups=mesh['ulysses'=8,'frame'=16,'quarter'=4] {'ulysses'}, dimensions={0} | all-to-all | bytes 1966080 | tf_op jit(solution)/shard_map/all_to_all | solution.py:131
  317.2 0.8 copy.96
  318.0 1.4 copy.97
  (61 shorter events, 2.2 us)
Async XLA Ops:
  0.0 115.7 %copy-start = (s32[40,768,5]{1,0,2:T(8,128)S(1)}, s32[40,768,5]{1,0,2:T(8,128)}, u32[]{:S(2)}) copy-start(s32[40,768,5]{1,0,2:T(8,128)} %param.15) | copy-start | bytes 1843204
  97.8 1.6 copy-start.6
  99.4 11.8 %copy-start.2 = (f32[40]{0:T(128)S(1)}, f32[40]{0:T(128)}, u32[]{:S(2)}) copy-start(f32[40]{0:T(128)} %param.19) | copy-start | bytes 484
  99.4 12.5 %copy-start.3 = (f32[40]{0:T(128)S(1)}, f32[40]{0:T(128)}, u32[]{:S(2)}) copy-start(f32[40]{0:T(128)} %param.18) | copy-start | bytes 484
  101.6 10.9 %copy-start.4 = (f32[40]{0:T(128)S(1)}, f32[40]{0:T(128)}, u32[]{:S(2)}) copy-start(f32[40]{0:T(128)} %param.17) | copy-start | bytes 484
  101.6 11.6 %copy-start.5 = (s32[40]{0:T(128)S(1)}, s32[40]{0:T(128)}, u32[]{:S(2)}) copy-start(s32[40]{0:T(128)} %param.14) | copy-start | bytes 484
  101.6 12.4 %copy-start.9 = (s32[40,768]{1,0:T(8,128)S(1)}, s32[40,768]{1,0:T(8,128)}, u32[]{:S(2)}) copy-start(s32[40,768]{1,0:T(8,128)} %param.16) | copy-start | bytes 368644
  101.6 100.5 %all-to-all-start.1 = ((bf16[16,48,15,128]{3,1,2,0:T(8,128)(2,1)}), bf16[16,48,15,128]{3,1,2,0:T(8,128)(2,1)}, u32[]{:S(2)}, u32[]{:S(2)}) async-start(bf16[16,48,15,128]{3,1,2,0:T(8,128)(2,1)} %copy.79), calls=%async_computation.1 | async-start | bytes 5898240 | tf_op jit(solution)/shard_map/all_to_all | solution.py:94
  119.8 97.6 %collective-permute-start.2 = (bf16[128,10,128]{2,0,1:T(8,128)(2,1)S(1)}, bf16[128,10,128]{2,0,1:T(8,128)(2,1)S(1)}, u32[]{:S(2)}, u32[]{:S(2)}) collective-permute-start(bf16[128,10,128]{2,0,1:T(8,128)(2,1)S(1)} %get-tuple-element.10), channel_id=1, source_target_pairs={{0,1},{1,2},{2,3},{3,4},{4,5},{5,6},{6,7},{7,8},{8,9},{9,10},{10,1... | collective-permute-start | bytes 983048 | tf_op jit(solution)/shard_map/ppermute | solution.py:15
  121.7 95.7 %collective-permute-start.3 = (bf16[128,10,128]{2,0,1:T(8,128)(2,1)S(1)}, bf16[128,10,128]{2,0,1:T(8,128)(2,1)S(1)}, u32[]{:S(2)}, u32[]{:S(2)}) collective-permute-start(bf16[128,10,128]{2,0,1:T(8,128)(2,1)S(1)} %get-tuple-element.11), channel_id=1, source_target_pairs={{1,0},{2,1},{3,2},{4,3},{5,4},{6,5},{7,6},{8,7},{9,8},{10,9},{11,1... | collective-permute-start | bytes 983048 | tf_op jit(solution)/shard_map/ppermute | solution.py:16
  204.7 1.6 copy-start.7
  206.3 21.7 %collective-permute-start = (bf16[128,10,128]{2,0,1:T(8,128)(2,1)S(1)}, bf16[128,10,128]{2,0,1:T(8,128)(2,1)S(1)}, u32[]{:S(2)}, u32[]{:S(2)}) collective-permute-start(bf16[128,10,128]{2,0,1:T(8,128)(2,1)S(1)} %get-tuple-element.12), channel_id=1, source_target_pairs={{0,4},{4,8},{8,12},{12,16},{16,20},{20,24},{24,28},{28,32},{32,36}... | collective-permute-start | bytes 983048 | tf_op jit(solution)/shard_map/ppermute | solution.py:15
  208.2 26.7 %collective-permute-start.1 = (bf16[128,10,128]{2,0,1:T(8,128)(2,1)S(1)}, bf16[128,10,128]{2,0,1:T(8,128)(2,1)S(1)}, u32[]{:S(2)}, u32[]{:S(2)}) collective-permute-start(bf16[128,10,128]{2,0,1:T(8,128)(2,1)S(1)} %get-tuple-element.13), channel_id=1, source_target_pairs={{4,0},{8,4},{12,8},{16,12},{20,16},{24,20},{28,24},{32,28},{36,32}... | collective-permute-start | bytes 983048 | tf_op jit(solution)/shard_map/ppermute | solution.py:16
  213.5 2.4 copy-start.8
  286.4 32.9 %copy-start.1 = (s32[40,768,5]{1,0,2:T(8,128)S(1)}, s32[40,768,5]{1,0,2:T(8,128)}, u32[]{:S(2)}) copy-start(s32[40,768,5]{1,0,2:T(8,128)} %param.15) | copy-start | bytes 1843204
